TPU v7x, 256 devices: a whole 4x4x8 slice. The times are simulated.
256 devices in a mesh: row: 4 (over y), col: 4 (over x), dp: 16 (over z, core).
Axes of the slice: x: 4, y: 4, z: 8, core: 2. Of those that a mesh axis runs over, the one named last changes fastest.
Arguments:
- hidden_states: bfloat16 [16384, 1536], P(('dp', 'row'), 'col'), may hold values from -18 to 18
- w_query: bfloat16 [1536, 1536], P('col', 'row'), may hold values from -0.102062073 to 0.102062073
- w_key_value: bfloat16 [1536, 512], P('col'), may hold values from -0.102062073 to 0.102062073
- adapter_down: bfloat16 [1024, 1536, 16], P('dp', 'col'), may hold values from -0.15625 to 0.15625
- adapter_up: bfloat16 [1024, 16, 1536], P('dp', None, 'row'), may hold values from -1.5 to 1.5
- req_lengths: int32 [16, 8], replicated, may hold values from 1 to 160, 960 in all within a row
- req_adapter: int32 [16, 8], replicated, may hold values from 0 to 1023, as said below
Outputs:
- attention: bfloat16 [16384, 1536], P(('dp', 'col'), 'row')
- kv_cache: bfloat16 [16384, 512], P(('dp', 'col'))
Inputs may be any that keep to these rules, and one draw needn't show every extreme that they name: `req_lengths`: the lengths of one block sum to 960, and each block has a request of exactly 160 tokens. `req_adapter`: adapters k * 64 to (k + 1) * 64 - 1 are those of index k of dp; the requests of one block use adapters of one index of dp at most 1 times, and some index of dp is used exactly that often by every block.
All inputs are finite; a program needn't handle non-finite values.
Results may differ from a plain program's by a relative error of at most 0.0072.
Values may be sent and summed in bfloat16 or wider, within the bound.
No kernel may reach another device: no remote copies, remote signals or barrier semaphores. Data moves between devices by JAX's collectives and lax.ppermute only.
A program may use at most 128 MiB of HBM per device.

v0:
```python
import math
import jax
import jax.numpy as jnp
from jax import lax
from jax.sharding import PartitionSpec as P

HEAD_DIM = 128
MOST_LEN = 160
masked_score = -1e30


def block_layout(lengths_row, block_len):
    prefix_len = block_len - jnp.sum(lengths_row)
    ends_at = jnp.cumsum(lengths_row) + prefix_len
    starts = ends_at - lengths_row
    positions = jnp.arange(block_len, dtype=jnp.int32)
    segment = jnp.sum((positions[:, None] >= starts[None, :]).astype(jnp.int32), axis=1)
    return (starts, segment, positions)


def slot_numbers(holders):
    request_total = holders.shape[0]
    ordering = jnp.arange(request_total, dtype=jnp.int32)
    earlier = ordering[None, :] < ordering[:, None]
    same_holder = holders[:, None] == holders[None, :]
    return jnp.sum((earlier & same_holder).astype(jnp.int32), axis=1)


def make_attend(query_rows, segment, first_row, kv_group, head_size, kv_half):
    own_rows = query_rows.shape[0]
    heads_here = query_rows.shape[1] // head_size
    query_heads = query_rows.reshape(own_rows, heads_here, head_size)
    query_pos = first_row + jnp.arange(own_rows, dtype=jnp.int32)
    query_seg = lax.dynamic_slice_in_dim(segment, first_row, own_rows, 0)
    score_scale = 1.0 / math.sqrt(head_size)

    def attend(state_in, key_block, key_start):
        running_max, running_sum, running_out = state_in
        block_size = key_block.shape[0]
        key_rows = lax.dynamic_slice_in_dim(key_block, kv_group * head_size, head_size, 1)
        values = lax.dynamic_slice_in_dim(key_block, kv_half + kv_group * head_size, head_size, 1)
        key_pos = jnp.arange(block_size, dtype=jnp.int32)
        allowed = (key_pos[None, :] <= query_pos[:, None]) & (
            (segment[None, :] == query_seg[:, None]) | (segment[None, :] == 0)
        )
        scores = (
            jnp.einsum("qhd,kd->hqk", query_heads, key_rows, preferred_element_type=jnp.float32)
            * score_scale
        )
        scores = jnp.where(allowed[None], scores, masked_score)
        new_max = jnp.maximum(running_max, jnp.max(scores, axis=2))
        weights = jnp.where(allowed[None], jnp.exp(scores - new_max[:, :, None]), 0.0)
        running_sum = jnp.sum(weights, axis=2)
        running_out = jnp.einsum(
            "hqk,kd->hqd", weights.astype(jnp.bfloat16), values, preferred_element_type=jnp.float32
        )
        return (new_max, running_sum, running_out)

    initial = (
        jnp.full((heads_here, own_rows), masked_score, jnp.float32),
        jnp.zeros((heads_here, own_rows), jnp.float32),
        jnp.zeros((heads_here, own_rows, head_size), jnp.float32),
    )
    return (attend, initial)


def body(hidden_states, w_query, w_key_value, adapter_down, adapter_up, req_lengths, req_adapter):
    dp_size = lax.axis_size("dp")
    block_index = lax.axis_index("dp")
    col_index = lax.axis_index("col")
    row_index = lax.axis_index("row")
    gathered = lax.all_gather(hidden_states, "row", axis=0, tiled=True)
    block_len = gathered.shape[0]
    query_cols = w_query.shape[1]
    kv_cols = w_key_value.shape[1]
    kv_half = kv_cols // 2
    head_size = HEAD_DIM
    heads_here = query_cols // head_size
    heads_total = heads_here * lax.axis_size("row")
    kv_heads = kv_half // head_size
    kv_group = row_index * heads_here // (heads_total // kv_heads)
    own_rows = block_len // lax.axis_size("col")
    first_row = col_index * own_rows
    held_sets = adapter_down.shape[0]
    width_here = adapter_down.shape[1]
    rank_size = adapter_down.shape[2]
    lengths_row = req_lengths[block_index]
    adapters_row = req_adapter[block_index]
    requests = lengths_row.shape[0]
    starts, segment, positions = block_layout(lengths_row, block_len)
    request_of = jnp.clip(segment - 1, 0, requests - 1)
    in_request = segment > 0
    holders = adapters_row // held_sets
    wanted_from_me = req_adapter // held_sets == block_index
    local_pick = jnp.sum(jnp.where(wanted_from_me, req_adapter % held_sets, 0), axis=1)
    down_pick = jnp.transpose(jnp.take(adapter_down, local_pick, axis=0), (0, 2, 1))
    up_pick = jnp.take(adapter_up, local_pick, axis=0)
    outgoing = jnp.concatenate([down_pick, up_pick], axis=1)
    incoming = lax.all_to_all(outgoing, "dp", split_axis=0, concat_axis=0, tiled=True)
    flat_down = incoming[:, :rank_size, :].reshape(dp_size * rank_size, width_here).T
    flat_up = (
        incoming[:, rank_size:, :].reshape(dp_size * rank_size, query_cols).astype(jnp.float32)
    )
    rank_owner = jnp.arange(dp_size * rank_size, dtype=jnp.int32) // rank_size
    reduced = jnp.dot(gathered, flat_down, preferred_element_type=jnp.float32)
    request_ids = jnp.arange(requests, dtype=jnp.int32)
    token_holder = (
        jnp.sum(
            jnp.where(segment[:, None] == request_ids[None, :] + 1, holders[None, :] + 1, 0), axis=1
        )
        - 1
    )
    kept_cols = rank_owner[None, :] == token_holder[:, None]
    reduced = jnp.where(kept_cols, reduced, 0.0)
    adapter_term = jnp.dot(reduced, flat_up, precision=lax.Precision.HIGHEST)
    kv_share = kv_cols // lax.axis_size("row")
    kv_slice = lax.dynamic_slice_in_dim(w_key_value, row_index * kv_share, kv_share, 1)
    both_weights = jnp.concatenate([w_query, kv_slice], axis=1)
    partial_value = jnp.dot(gathered, both_weights, preferred_element_type=jnp.float32)
    summed = lax.psum_scatter(
        partial_value
        + jnp.concatenate(
            [adapter_term, jnp.zeros((own_rows * lax.axis_size("col"), kv_share), jnp.float32)],
            axis=1,
        ),
        "col",
        scatter_dimension=0,
        tiled=True,
    )
    query_rows = summed[:, :query_cols].astype(jnp.bfloat16)
    kv_pieces = lax.all_gather(summed[:, query_cols:].astype(jnp.bfloat16), ("row", "col"), axis=0)
    kv_pieces = kv_pieces.reshape(lax.axis_size("row"), lax.axis_size("col"), own_rows, kv_share)
    own_pieces = lax.dynamic_index_in_dim(kv_pieces, col_index, 1, keepdims=False)
    kv_cache = jnp.transpose(own_pieces, (1, 0, 2)).reshape(own_rows, kv_cols)
    parts_per_head = head_size // kv_share
    key_all = lax.dynamic_slice_in_dim(kv_pieces, kv_group * parts_per_head, parts_per_head, 0)
    value_all = lax.dynamic_slice_in_dim(
        kv_pieces, (kv_heads + kv_group) * parts_per_head, parts_per_head, 0
    )
    key_all = jnp.transpose(key_all, (1, 2, 0, 3)).reshape(block_len, head_size)
    value_all = jnp.transpose(value_all, (1, 2, 0, 3)).reshape(block_len, head_size)
    attend, initial = make_attend(query_rows, segment, first_row, 0, head_size, head_size)
    running_max, running_sum, running_out = attend(
        initial, jnp.concatenate([key_all, value_all], axis=1), jnp.int32(0)
    )
    attention = (running_out / running_sum[:, :, None]).astype(jnp.bfloat16)
    attention = jnp.transpose(attention, (1, 0, 2)).reshape(own_rows, query_cols)
    return (attention, kv_cache)


def solution(mesh):
    return jax.shard_map(
        body,
        mesh=mesh,
        in_specs=(
            P(("dp", "row"), "col"),
            P("col", "row"),
            P("col", None),
            P("dp", "col", None),
            P("dp", None, "row"),
            P(),
            P(),
        ),
        out_specs=(P(("dp", "col"), "row"), P(("dp", "col"), None)),
        check_vma=False,
    )
```

profile of v0, /device:TPU:2, one launch (start us, length us, event | category | flops | bytes accessed | tf_op | source)
XLA Modules:
  0.0 139.3 jit_solution(9572171960682573029)
XLA Ops:
  7.2 0.0 copy-start
  7.2 0.0 copy-start.3
  7.2 0.0 copy-start.4
  7.2 0.0 copy-start.2
  7.2 0.8 fusion.25
  8.0 0.3 copy-done
  8.3 0.6 gather_fusion.1
  8.9 1.7 %gather_fusion = bf16[16,384,16]{1,2,0:T(8,128)(2,1)S(1)} fusion(bf16[64,384,16]{1,2,0:T(8,128)(2,1)} %param.10, s32[1024]{0:T(1024)S(1)} %pad_clamp_fusion), kind=kCustom, calls=%fused_computation | custom fusion | bytes 393280 | tf_op jit(solution)/shard_map/jit(_take)/gather | solution.py:96
  10.6 0.1 broadcast_select_fusion
  10.7 0.1 select_bitcast_fusion
  10.9 0.8 pad_maximum_fusion
  11.6 8.6 %all-to-all-start = ((bf16[16,32,384]{2,1,0:T(8,128)(2,1)}), bf16[16,32,384]{2,1,0:T(8,128)(2,1)S(1)}, u32[]{:S(2)}, u32[]{:S(2)}) async-start(bf16[16,32,384]{2,1,0:T(8,128)(2,1)} %pad_maximum_fusion), calls=%async_computation | async-start | bytes 786432 | tf_op jit(solution)/shard_map/all_to_all | solution.py:99
  20.2 0.0 reduce-scatter.2.cloned.1.call-start
  20.3 0.0 copy-done.3
  20.3 0.0 copy-done.4
  20.3 0.7 fusion.34
  21.7 0.1 subtract_reduce_fusion
  21.8 0.1 convert_reduce_fusion
  21.9 0.9 constant_dynamic-slice_fusion.3
  22.8 0.1 select_reduce_fusion
  22.9 0.0 copy-done.2
  22.9 0.0 copy-start.1
  22.9 14.5 %all_gather.9 = bf16[1024,384]{1,0:T(8,128)(2,1)S(1)} all-gather(bf16[256,384]{1,0:T(8,128)(2,1)S(1)} %copy-done.2), channel_id=1, replica_groups=mesh['row'=4,'col'=4,'dp'=16] {'row'}, dimensions={0}, use_global_device_ids=true | all-gather | bytes 983040 | tf_op jit(solution)/shard_map/all_gather | solution.py:72
  37.4 0.0 all-to-all-done
  37.4 0.5 fusion.6
  37.9 0.9 fusion.36
  38.8 0.0 copy-done.1
  38.8 2.1 %bitcast_add_fusion = f32[1024,512]{0,1:T(8,128)} fusion(f32[1024,384]{0,1:T(8,128)S(1)} %fusion.36, bf16[1024,384]{1,0:T(8,128)(2,1)S(1)} %all_gather.9, bf16[384,128]{1,0:T(8,128)(2,1)S(1)} %constant_dynamic-slice_fusion.3, bf16[384,384]{1,0:T(8,128)(2,1)S(1)} %copy-done.1), kind=kOutput, calls=%fused_computation.7 | convolution fusion | flops 403963904 | bytes 4849664 | tf_op jit(solution)/shard_map/dot_general | solution.py:119
  40.9 0.0 reduce-scatter.2.cloned.1.call-update
  41.0 0.0 all-gather.3.cloned.1.call-start
  41.0 32.3 %reduce-scatter.2.cloned.1.call-done = f32[256,512]{0,1:T(8,128)} async-done(((f32[1024,512]{0,1:T(8,128)}), f32[256,512]{0,1:T(8,128)}) %reduce-scatter.2.cloned.1.call-update) | async-done | bytes 524304 | tf_op jit(solution)/shard_map/reduce_scatter | solution.py:120
  73.3 1.1 convert.4
  74.4 0.6 slice.24
  75.0 0.0 all-gather.3.cloned.1.call-update
  75.1 0.1 dynamic_slice.23
  75.2 0.8 fusion.10
  76.0 49.1 %all-gather.3.cloned.1.call-done = bf16[4096,128]{0,1:T(8,128)(2,1)} async-done(((bf16[256,128]{0,1:T(8,128)(2,1)}), bf16[4096,128]{0,1:T(8,128)(2,1)}) %all-gather.3.cloned.1.call-update) | async-done | bytes 1048592 | tf_op jit(solution)/shard_map/all_gather | solution.py:131
  125.1 1.8 %reshape.151 = bf16[4,4,256,128]{2,1,0,3:T(4,128)(2,1)S(1)} reshape(bf16[4096,128]{0,1:T(8,128)(2,1)} %all-gather.3.cloned.1.call-done) | data formatting | bytes 2097152 | tf_op jit(solution)/shard_map/reshape | solution.py:132
  127.0 0.5 constant_dynamic-slice_fusion.2
  127.6 0.1 copy.40
  127.6 0.8 copy.35
  128.5 0.2 constant_dynamic-slice_fusion.1
  128.7 0.2 copy.29
  128.9 0.2 reshape.174
  129.1 0.7 fusion
  129.8 0.8 fusion.1
  130.6 1.0 fusion.14
  131.6 0.8 copy.34
  (12 shorter events, 0.1 us)
Async XLA Ops:
  7.2 1.2 copy-start
  7.2 13.1 %copy-start.3 = (s32[16,8]{0,1:T(8,128)S(1)}, s32[16,8]{0,1:T(8,128)}, u32[]{:S(2)}) copy-start(s32[16,8]{0,1:T(8,128)} %param.13) | copy-start | bytes 1540
  7.2 13.1 %copy-start.4 = (s32[16,8]{0,1:T(8,128)S(1)}, s32[16,8]{0,1:T(8,128)}, u32[]{:S(2)}) copy-start(s32[16,8]{0,1:T(8,128)} %param.12) | copy-start | bytes 1540
  7.2 15.7 %copy-start.2 = (bf16[256,384]{1,0:T(8,128)(2,1)S(1)}, bf16[256,384]{1,0:T(8,128)(2,1)}, u32[]{:S(2)}) copy-start(bf16[256,384]{1,0:T(8,128)(2,1)} %param.7) | copy-start | bytes 589828
  11.6 25.8 %all-to-all-start = ((bf16[16,32,384]{2,1,0:T(8,128)(2,1)}), bf16[16,32,384]{2,1,0:T(8,128)(2,1)S(1)}, u32[]{:S(2)}, u32[]{:S(2)}) async-start(bf16[16,32,384]{2,1,0:T(8,128)(2,1)} %pad_maximum_fusion), calls=%async_computation | async-start | bytes 786432 | tf_op jit(solution)/shard_map/all_to_all | solution.py:99
  20.2 53.1 %reduce-scatter.2.cloned.1.call-start = ((), (), s32[]{:S(2)}) async-start(), calls=%async_computation.2 | async-start | bytes 2621440 | tf_op jit(solution)/shard_map/reduce_scatter | solution.py:120
  22.9 15.9 %copy-start.1 = (bf16[384,384]{1,0:T(8,128)(2,1)S(1)}, bf16[384,384]{1,0:T(8,128)(2,1)}, u32[]{:S(2)}) copy-start(bf16[384,384]{1,0:T(8,128)(2,1)} %param.8) | copy-start | bytes 884740
  41.0 84.2 %all-gather.3.cloned.1.call-start = ((), (), s32[]{:S(2)}) async-start(), calls=%async_computation.3 | async-start | bytes 1114112 | tf_op jit(solution)/shard_map/all_gather | solution.py:131
Sparse Core Ops, SparseCore 0:
  41.1 32.1 reduce-scatter.1
  76.3 48.8 all-gather.2
where the time goes:
time: 140 us; the launch traced here: 139 us
  waiting for transfers between devices  81.5 us (58%)
  between operations  15 us (11%)
  blocking collectives  14.5 us (10%)
  local copies, waits for them, and re-layouts  9.02 us (6%)
  starting transfers between devices  8.65 us (6%)
  other arithmetic  5.54 us (4%)
  matrix products  5.16 us (4%)
    all_gather x1, waiting for transfers between devices, body(): lax.all_gather(summed[:, query_cols:].astype(jnp.bfloat16), ('row', 'col'...  49.1 us
    reduce_scatter x1, waiting for transfers between devices, body(): lax.psum_scatter(partial_value + jnp.concatenate([adapter_term, jnp.zeros...  32.3 us
    all_gather x1, blocking collectives, body(): gathered = lax.all_gather(hidden_states, 'row', axis=0, tiled=True)  14.5 us
    all_to_all x1, starting transfers between devices, body(): lax.all_to_all(outgoing, 'dp', split_axis=0, concat_axis=0, tiled=True)  8.57 us
  transfers between devices with their start and end apart: 3, of which 2 were waited for; matrix products, arithmetic and copies ran while one was open for 2% of the time, Pallas kernels for 0%

commit v1 on v0

--- a/solution.py
+++ b/solution.py
@@ -69,7 +69,20 @@
     block_index = lax.axis_index("dp")
     col_index = lax.axis_index("col")
     row_index = lax.axis_index("row")
-    gathered = lax.all_gather(hidden_states, "row", axis=0, tiled=True)
+
+    def feed_ladders(sample, link_axis):
+        all_values = jnp.concatenate(
+            lax.all_to_all(
+                jnp.stack(tuple((sample for _ in range(lax.axis_size(link_axis))))),
+                axis_name=link_axis,
+                split_axis=0,
+                concat_axis=0,
+            ),
+            axis=0,
+        )
+        return all_values
+
+    gathered = feed_ladders(hidden_states, link_axis="row")
     block_len = gathered.shape[0]
     query_cols = w_query.shape[1]
     kv_cols = w_key_value.shape[1]

time: 140 us -> 149 us (1.064)
  waiting for transfers between devices: 81.5 us -> 99.8 us
  blocking collectives: 14.5 us -> 0 us
  starting transfers between devices: 8.65 us -> 13.1 us
    all_gather x1 -> x0, blocking collectives: 14.5 us -> none  [body(): gathered = lax.all_gather(hidden_states, 'row', axis=0, tiled=True)]
    all_to_all x0 -> x1, waiting for transfers between devices: none -> 13.5 us  [feed_ladders(): lax.all_to_all(jnp.stack(tuple((sample for _ in range(lax.axis_size(link_...]
    all_to_all x1, waiting for transfers between devices: 0.01 us -> 11.1 us  [body(): lax.all_to_all(outgoing, 'dp', split_axis=0, concat_axis=0, tiled=True)]
    reduce_scatter x1, waiting for transfers between devices: 32.3 us -> 26.1 us  [body(): lax.psum_scatter(partial_value + jnp.concatenate([adapter_term, jnp.zeros...]
    all_to_all x0 -> x1, starting transfers between devices: none -> 4.46 us  [feed_ladders(): lax.all_to_all(jnp.stack(tuple((sample for _ in range(lax.axis_size(link_...]
  transfers between devices with their start and end apart: 3 -> 4, of which waited for: 2 -> 4; matrix products, arithmetic and copies ran while one was open for 2% -> 2% of each run, Pallas kernels for 0% -> 0%
where the time goes in v1:
time: 149 us
  waiting for transfers between devices  99.8 us (67%)
  between operations  15 us (10%)
  starting transfers between devices  13.1 us (9%)
  local copies, waits for them, and re-layouts  9.96 us (7%)
  other arithmetic  5.54 us (4%)
  matrix products  5.16 us (3%)
    all_gather x1, waiting for transfers between devices, body(): lax.all_gather(summed[:, query_cols:].astype(jnp.bfloat16), ('row', 'col'...  49.2 us
    reduce_scatter x1, waiting for transfers between devices, body(): lax.psum_scatter(partial_value + jnp.concatenate([adapter_term, jnp.zeros...  26.1 us
    all_to_all x1, waiting for transfers between devices, feed_ladders(): lax.all_to_all(jnp.stack(tuple((sample for _ in range(lax.axis_size(link_...  13.5 us
    all_to_all x1, waiting for transfers between devices, body(): lax.all_to_all(outgoing, 'dp', split_axis=0, concat_axis=0, tiled=True)  11.1 us
    all_to_all x1, starting transfers between devices, body(): lax.all_to_all(outgoing, 'dp', split_axis=0, concat_axis=0, tiled=True)  8.57 us
    all_to_all x1, starting transfers between devices, feed_ladders(): lax.all_to_all(jnp.stack(tuple((sample for _ in range(lax.axis_size(link_...  4.46 us
  transfers between devices with their start and end apart: 4, of which 4 were waited for; matrix products, arithmetic and copies ran while one was open for 2% of the time, Pallas kernels for 0%

profile of v1, /device:TPU:2, one launch (start us, length us, event | category | flops | bytes accessed | tf_op | source)
XLA Modules:
  0.0 148.5 jit_solution(4222879028124026218)
XLA Ops:
  7.2 0.0 copy-start
  7.2 0.0 copy-start.3
  7.2 0.0 copy-start.4
  7.2 0.0 copy-start.2
  7.2 0.8 fusion.25
  8.0 0.3 copy-done
  8.3 0.6 gather_fusion.1
  8.9 1.7 %gather_fusion = bf16[16,384,16]{1,2,0:T(8,128)(2,1)S(1)} fusion(bf16[64,384,16]{1,2,0:T(8,128)(2,1)} %param.10, s32[1024]{0:T(1024)S(1)} %pad_clamp_fusion), kind=kCustom, calls=%fused_computation | custom fusion | bytes 393280 | tf_op jit(solution)/shard_map/jit(_take)/gather | solution.py:109
  10.6 0.1 broadcast_select_fusion
  10.7 0.1 select_bitcast_fusion
  10.9 0.8 pad_maximum_fusion
  11.6 8.6 %all-to-all-start.1 = ((bf16[16,32,384]{2,1,0:T(8,128)(2,1)}), bf16[16,32,384]{2,1,0:T(8,128)(2,1)S(1)}, u32[]{:S(2)}, u32[]{:S(2)}) async-start(bf16[16,32,384]{2,1,0:T(8,128)(2,1)} %pad_maximum_fusion), calls=%async_computation.1 | async-start | bytes 786432 | tf_op jit(solution)/shard_map/all_to_all | solution.py:112
  20.2 0.0 copy-done.3
  20.2 0.0 copy-done.4
  20.2 0.7 fusion.34
  21.7 0.1 subtract_reduce_fusion
  21.8 0.1 convert_reduce_fusion
  21.9 0.9 constant_dynamic-slice_fusion.3
  22.8 11.1 %all-to-all-done.1 = bf16[16,32,384]{2,1,0:T(8,128)(2,1)S(1)} async-done(((bf16[16,32,384]{2,1,0:T(8,128)(2,1)}), bf16[16,32,384]{2,1,0:T(8,128)(2,1)S(1)}, u32[]{:S(2)}, u32[]{:S(2)}) %all-to-all-start.1) | async-done | bytes 393248 | tf_op jit(solution)/shard_map/all_to_all | solution.py:112
  33.8 0.0 copy-done.2
  33.8 0.9 stack.2
  34.8 4.5 %all-to-all-start = ((bf16[4,256,384]{2,1,0:T(8,128)(2,1)}), bf16[4,256,384]{2,1,0:T(8,128)(2,1)S(1)}, u32[]{:S(2)}, u32[]{:S(2)}) async-start(bf16[4,256,384]{2,1,0:T(8,128)(2,1)} %stack.2), calls=%async_computation | async-start | bytes 1572864 | tf_op jit(solution)/shard_map/all_to_all | solution.py:75
  39.3 0.0 reduce-scatter.2.cloned.1.call-start
  39.3 0.1 select_reduce_fusion
  39.4 13.5 %all-to-all-done = bf16[4,256,384]{2,1,0:T(8,128)(2,1)S(1)} async-done(((bf16[4,256,384]{2,1,0:T(8,128)(2,1)}), bf16[4,256,384]{2,1,0:T(8,128)(2,1)S(1)}, u32[]{:S(2)}, u32[]{:S(2)}) %all-to-all-start) | async-done | bytes 786464 | tf_op jit(solution)/shard_map/all_to_all | solution.py:75
  52.9 0.5 fusion.6
  53.4 0.9 fusion.36
  54.3 2.1 %bitcast_add_fusion = f32[1024,512]{0,1:T(8,128)} fusion(f32[1024,384]{0,1:T(8,128)S(1)} %fusion.36, bf16[1024,384]{1,0:T(8,128)(2,1)S(1)} %bitcast.63, bf16[384,128]{1,0:T(8,128)(2,1)S(1)} %constant_dynamic-slice_fusion.3, bf16[384,384]{1,0:T(8,128)(2,1)S(1)} %copy-done.1), kind=kOutput, calls=%fused_computation.7 | convolution fusion | flops 403963904 | bytes 4849664 | tf_op jit(solution)/shard_map/dot_general | solution.py:132
  56.4 0.0 reduce-scatter.2.cloned.1.call-update
  56.5 0.0 all-gather.3.cloned.1.call-start
  56.5 26.1 %reduce-scatter.2.cloned.1.call-done = f32[256,512]{0,1:T(8,128)} async-done(((f32[1024,512]{0,1:T(8,128)}), f32[256,512]{0,1:T(8,128)}) %reduce-scatter.2.cloned.1.call-update) | async-done | bytes 524304 | tf_op jit(solution)/shard_map/reduce_scatter | solution.py:133
  82.6 1.1 convert.4
  83.6 0.6 slice.24
  84.3 0.0 all-gather.3.cloned.1.call-update
  84.3 0.1 dynamic_slice.23
  84.4 0.8 fusion.10
  85.3 49.2 %all-gather.3.cloned.1.call-done = bf16[4096,128]{0,1:T(8,128)(2,1)} async-done(((bf16[256,128]{0,1:T(8,128)(2,1)}), bf16[4096,128]{0,1:T(8,128)(2,1)}) %all-gather.3.cloned.1.call-update) | async-done | bytes 1048592 | tf_op jit(solution)/shard_map/all_gather | solution.py:144
  134.4 1.8 %reshape.157 = bf16[4,4,256,128]{2,1,0,3:T(4,128)(2,1)S(1)} reshape(bf16[4096,128]{0,1:T(8,128)(2,1)} %all-gather.3.cloned.1.call-done) | data formatting | bytes 2097152 | tf_op jit(solution)/shard_map/reshape | solution.py:145
  136.3 0.5 constant_dynamic-slice_fusion.2
  136.8 0.1 copy.40
  136.9 0.8 copy.35
  137.8 0.2 constant_dynamic-slice_fusion.1
  137.9 0.2 copy.29
  138.2 0.2 reshape.180
  138.4 0.7 fusion
  139.1 0.8 fusion.1
  139.9 1.0 fusion.14
  140.9 0.8 copy.34
  (14 shorter events, 0.1 us)
Async XLA Ops:
  7.2 1.2 copy-start
  7.2 13.0 %copy-start.3 = (s32[16,8]{0,1:T(8,128)S(1)}, s32[16,8]{0,1:T(8,128)}, u32[]{:S(2)}) copy-start(s32[16,8]{0,1:T(8,128)} %param.13) | copy-start | bytes 1540
  7.2 13.0 %copy-start.4 = (s32[16,8]{0,1:T(8,128)S(1)}, s32[16,8]{0,1:T(8,128)}, u32[]{:S(2)}) copy-start(s32[16,8]{0,1:T(8,128)} %param.12) | copy-start | bytes 1540
  7.2 26.6 %copy-start.2 = (bf16[256,384]{1,0:T(8,128)(2,1)S(1)}, bf16[256,384]{1,0:T(8,128)(2,1)}, u32[]{:S(2)}) copy-start(bf16[256,384]{1,0:T(8,128)(2,1)} %param.7) | copy-start | bytes 589828
  11.6 22.2 %all-to-all-start.1 = ((bf16[16,32,384]{2,1,0:T(8,128)(2,1)}), bf16[16,32,384]{2,1,0:T(8,128)(2,1)S(1)}, u32[]{:S(2)}, u32[]{:S(2)}) async-start(bf16[16,32,384]{2,1,0:T(8,128)(2,1)} %pad_maximum_fusion), calls=%async_computation.1 | async-start | bytes 786432 | tf_op jit(solution)/shard_map/all_to_all | solution.py:112
  34.8 18.1 %all-to-all-start = ((bf16[4,256,384]{2,1,0:T(8,128)(2,1)}), bf16[4,256,384]{2,1,0:T(8,128)(2,1)S(1)}, u32[]{:S(2)}, u32[]{:S(2)}) async-start(bf16[4,256,384]{2,1,0:T(8,128)(2,1)} %stack.2), calls=%async_computation | async-start | bytes 1572864 | tf_op jit(solution)/shard_map/all_to_all | solution.py:75
  39.3 15.0 %copy-start.1 = (bf16[384,384]{1,0:T(8,128)(2,1)S(1)}, bf16[384,384]{1,0:T(8,128)(2,1)}, u32[]{:S(2)}) copy-start(bf16[384,384]{1,0:T(8,128)(2,1)} %param.8) | copy-start | bytes 884740
  39.3 43.3 %reduce-scatter.2.cloned.1.call-start = ((), (), s32[]{:S(2)}) async-start(), calls=%async_computation.3 | async-start | bytes 2621440 | tf_op jit(solution)/shard_map/reduce_scatter | solution.py:133
  56.5 78.0 %all-gather.3.cloned.1.call-start = ((), (), s32[]{:S(2)}) async-start(), calls=%async_computation.4 | async-start | bytes 1114112 | tf_op jit(solution)/shard_map/all_gather | solution.py:144
Sparse Core Ops, SparseCore 0:
  56.6 25.9 reduce-scatter.1
  85.6 48.8 all-gather.2
